TPU v7x, 256 devices: a whole 4x4x8 slice. The times are simulated.
256 devices in a mesh: dp: 32 (over x, z_hi, y), owner: 8 (over z_lo, core).
Axes of the slice: x: 4, y: 4, z: 8 (z_hi: 2, z_lo: 4; z = z_hi * 4 + z_lo), core: 2. Of those that a mesh axis runs over, the one named last changes fastest.
Arguments:
- line_columns: bfloat16 [8, 131072, 512], P(None, ('dp', 'owner')), may hold values from -12 to 12
- line_widths: int32 [256, 4], P(('dp', 'owner')), may hold values from 1 to 128, as said below
- layer_owner: int32 [8], replicated, may hold values from 0 to 7, each once
Outputs:
- preconditioned: float32 [8, 1152, 128], replicated
Inputs may be any that keep to these rules, and one draw needn't show every extreme that they name: `line_widths`: row b holds the widths of the 4 lines of device b, laid end to end from its first position; in every draw the lines of some device all have width 128.
All inputs are finite; a program needn't handle non-finite values.
Results may differ from a plain program's by a relative error of at most 0.0003.
Values may be sent and summed in bfloat16 or wider, within the bound.
No kernel may reach another device: no remote copies, remote signals or barrier semaphores. Data moves between devices by JAX's collectives and lax.ppermute only.
A program may use at most 128 MiB of HBM per device.

v0:
```python
import numpy as np
import jax
import jax.numpy as jnp
from jax import lax
from jax.sharding import PartitionSpec as P

damping = 0.1


def patch_columns(block, widths):
    positions = block.shape[-2]
    channels = block.shape[-1] // 4
    line_ends = jnp.cumsum(widths, axis=-1).astype(jnp.int32)
    line_starts = line_ends - widths
    place = jnp.arange(positions, dtype=jnp.int32)[:, None]
    opening = jnp.any(place == line_starts[..., None, :], axis=-1)[..., None]
    closing = jnp.any(place + 1 == line_ends[..., None, :], axis=-1)[..., None]
    inside = place < line_ends[..., None, -1:]
    features = block[..., : 3 * channels]
    gradients = block[..., 3 * channels :]
    padding = jnp.zeros_like(features[..., :1, :])
    before = jnp.concatenate([padding, features[..., :-1, :]], axis=-2)
    after = jnp.concatenate([features[..., 1:, :], padding], axis=-2)
    before = jnp.where(opening, jnp.zeros_like(before), before)
    after = jnp.where(closing, jnp.zeros_like(after), after)
    stacked = jnp.concatenate([before, features, after, gradients], axis=-1)
    return jnp.where(inside, stacked, jnp.zeros_like(stacked))


def precondition(factor, total_rows):
    full_width = factor.shape[0]
    patch_width = full_width // 10 * 9
    scaled = factor / total_rows
    act_factor = scaled[:patch_width, :patch_width] + damping * jnp.eye(
        patch_width, dtype=factor.dtype
    )
    grad_factor = scaled[patch_width:, patch_width:] + damping * jnp.eye(
        full_width - patch_width, dtype=factor.dtype
    )
    cross_term = scaled[:patch_width, patch_width:]
    act_cholesky = jnp.linalg.cholesky(act_factor)
    left_solved = jax.scipy.linalg.cho_solve((act_cholesky, True), cross_term)
    grad_cholesky = jnp.linalg.cholesky(grad_factor)
    return jax.scipy.linalg.cho_solve((grad_cholesky, True), left_solved.T).T


def _tri_pairs(nb):
    return [(i, j) for i in range(nb) for j in range(i + 1)]


def pack_lower(gram, block):
    nb = gram.shape[0] // block
    tiles = gram.reshape(nb, block, nb, block).transpose(0, 2, 1, 3)
    pairs = _tri_pairs(nb)
    rows = np.array([p[0] for p in pairs], dtype=np.int32)
    cols = np.array([p[1] for p in pairs], dtype=np.int32)
    return tiles[rows, cols]


def unpack_lower(blocks, nb):
    block = blocks.shape[-1]
    index = {p: k for k, p in enumerate(_tri_pairs(nb))}
    pick = np.array(
        [[index[max(i, j), min(i, j)] for j in range(nb)] for i in range(nb)], dtype=np.int32
    )
    upper = np.array([[i < j for j in range(nb)] for i in range(nb)])
    tiles = blocks[pick]
    tiles = jnp.where(upper[:, :, None, None], jnp.swapaxes(tiles, -1, -2), tiles)
    return tiles.transpose(0, 2, 1, 3).reshape(nb * block, nb * block)


HIGH = lax.Precision.HIGHEST


def _mm(a, b):
    return jnp.dot(a, b, precision=HIGH, preferred_element_type=jnp.float32)


def _mm_t(a, b):
    return lax.dot_general(
        a, b, (((0,), (0,)), ((), ())), precision=HIGH, preferred_element_type=jnp.float32
    )


def _mm_nt(a, b):
    return lax.dot_general(
        a, b, (((1,), (1,)), ((), ())), precision=HIGH, preferred_element_type=jnp.float32
    )


def _chol_inv(block):
    lower = jnp.linalg.cholesky(block, symmetrize_input=False)
    eye = jnp.eye(block.shape[0], dtype=block.dtype)
    inverse = lax.linalg.triangular_solve(lower, eye, left_side=True, lower=True)
    return (lower, inverse)


def precondition_blocks(blocks, nb, total_rows):
    block = blocks.shape[-1]
    na = nb - 1
    index = {p: k for k, p in enumerate(_tri_pairs(nb))}
    zero = len(index)
    pick = np.array(
        [[index[i, j] if i >= j else zero for j in range(na)] for i in range(nb)], dtype=np.int32
    )
    scale = 1.0 / total_rows
    tiles = blocks[pick] * scale
    work = tiles.transpose(0, 2, 1, 3).reshape(nb * block, na * block)
    eye = jnp.eye(block, dtype=blocks.dtype)
    grad_factor = blocks[index[na, na]] * scale + damping * eye
    inverses = []
    for k in range(na):
        lo = k * block
        hi = lo + block
        diag = work[lo:hi, lo:hi] + damping * eye
        lower, inverse = _chol_inv(diag)
        inverses.append(inverse)
        panel = _mm_nt(work[hi:, lo:hi], inverse)
        work = work.at[lo:hi, lo:hi].set(lower)
        work = work.at[hi:, lo:hi].set(panel)
        if k + 1 < na:
            update = _mm_nt(panel, panel[: (na - k - 1) * block])
            work = work.at[hi:, hi:].add(-update)
    solved_t = work[na * block :, :]
    pieces = [None] * na
    for k in reversed(range(na)):
        lo = k * block
        hi = lo + block
        rhs = solved_t[:, lo:hi].T
        if k + 1 < na:
            below = jnp.concatenate(pieces[k + 1 :], axis=0)
            rhs = rhs - _mm_t(work[hi : na * block, lo:hi], below)
        pieces[k] = _mm_t(inverses[k], rhs)
    left_solved = jnp.concatenate(pieces, axis=0)
    _, grad_inverse = _chol_inv(grad_factor)
    return _mm(_mm_nt(left_solved, grad_inverse), grad_inverse)


def body(line_columns, line_widths, layer_owner):
    layer_count, positions, packed_width = line_columns.shape
    channels = packed_width // 4
    full_width = 10 * channels
    n_replicas = 1
    for axis in DP_AXES:
        n_replicas = n_replicas * lax.axis_size(axis)
    n_owners = lax.axis_size("owner")
    per_owner = layer_count // n_owners
    total_rows = n_replicas * n_owners * positions
    ordered = jnp.take(line_columns, layer_owner, axis=0)
    width_copies = jnp.broadcast_to(line_widths[None, :, :], (n_owners, 1, line_widths.shape[1]))
    received, source_widths = (
        lax.all_to_all(ordered, "owner", split_axis=0, concat_axis=1, tiled=True),
        lax.all_to_all(width_copies, "owner", split_axis=0, concat_axis=1, tiled=True),
    )
    blocks = received.reshape(per_owner, n_owners, positions, packed_width)
    columns = patch_columns(blocks, source_widths.reshape(n_owners, line_widths.shape[1]))
    columns = columns.reshape(n_owners * positions, full_width)
    gram = jnp.dot(columns.T, columns, preferred_element_type=jnp.float32)
    block = 128
    nb = full_width // block
    packed = pack_lower(gram, block)
    n_blocks = packed.shape[0]
    padded = -(-n_blocks * block // (8 * n_replicas)) * 8 * n_replicas // block
    packed = jnp.concatenate(
        [packed, jnp.zeros((padded - n_blocks, block, block), packed.dtype)], axis=0
    )
    chunk = padded * block // n_replicas
    packed = packed.reshape(n_replicas, chunk, block)
    mine = packed.reshape(padded * block, block)
    for axis in SCATTER_ORDER:
        mine = lax.psum_scatter(mine, axis, scatter_dimension=0, tiled=True)
    gathered = mine
    for axis in SCATTER_ORDER[::-1]:
        gathered = lax.all_gather(gathered, axis, axis=0, tiled=True)
    gathered = gathered.reshape(padded, block, block)
    results = precondition_blocks(gathered, nb, total_rows)[None]
    return lax.all_gather(results, "owner", axis=0, tiled=True)


DP_AXES = ("dp_x", "dp_z", "dp_y")
SCATTER_ORDER = ("dp_y", "dp_x", "dp_z")


def solution(mesh):
    dp_shape = (4, 2, mesh.shape["dp"] // 8)
    devices = mesh.devices.reshape(dp_shape + (mesh.shape["owner"],))
    fine = jax.sharding.Mesh(devices, DP_AXES + ("owner",))
    rows = DP_AXES + ("owner",)
    in_specs = (P(None, rows, None), P(rows, None), P())
    out_specs = P()
    return jax.shard_map(body, mesh=fine, in_specs=in_specs, out_specs=out_specs, check_vma=False)
```

profile of v0, /device:TPU:2, one launch (start us, length us, event | category | flops | bytes accessed | tf_op | source)
XLA Modules:
  0.0 770.8 jit_solution(15448216205919539234)
XLA Ops:
  7.8 5.9 all-to-all-start
  15.0 5.0 gather_fusion
  20.0 4.7 broadcast_select_fusion
  24.7 5.1 all-to-all-start.1
  30.2 93.7 %all-to-all-done.1 = bf16[8,512,512]{2,1,0:T(8,128)(2,1)} async-done(((bf16[8,512,512]{2,1,0:T(8,128)(2,1)}), bf16[8,512,512]{2,1,0:T(8,128)(2,1)}, u32[]{:S(2)}, u32[]{:S(2)}) %all-to-all-start.1) | async-done | bytes 4194336 | tf_op jit(solution)/shard_map/all_to_all | solution.py:152
  125.2 2.3 slice.830
  127.5 3.9 fusion.101
  131.3 2.2 pad_select_fusion
  133.6 6.0 fusion
  139.5 14.3 %copy.37 = bf16[1280,4096]{1,0:T(8,128)(2,1)} copy(bf16[1280,4096]{0,1:T(8,128)(2,1)} %fusion) | data formatting | bytes 20971520 | tf_op jit(solution)/shard_map/dot_general | solution.py:158
  153.9 22.7 %convolution_bitcast_fusion = f32[10,10,128,128]{3,2,1,0:T(8,128)} fusion(bf16[10,128,4096,1]{2,1,3,0:T(8,128)(2,1)} %bitcast.176, bf16[10,128,4096,1]{2,1,0,3:T(8,128)(2,1)} %bitcast.177), kind=kOutput, calls=%fused_computation.13 | convolution fusion | flops 13421772800 | bytes 27525120 | tf_op jit(solution)/shard_map/dot_general | solution.py:158
  176.6 5.5 gather_fusion.1
  182.0 4.3 concatenate.110
  186.4 45.5 %reduce-scatter.4.cloned.1.call-done = f32[1792,128]{1,0:T(8,128)} async-done(((f32[7168,128]{1,0:T(8,128)}), f32[1792,128]{1,0:T(8,128)}) %reduce-scatter.4.cloned.1.call-update) | async-done | bytes 917520 | tf_op jit(solution)/shard_map/reduce_scatter | solution.py:171
  232.1 25.5 %reduce-scatter.6.cloned.1.call-done = f32[448,128]{1,0:T(8,128)} async-done(((f32[1792,128]{1,0:T(8,128)}), f32[448,128]{1,0:T(8,128)}) %reduce-scatter.6.cloned.1.call-update) | async-done | bytes 229392 | tf_op jit(solution)/shard_map/reduce_scatter | solution.py:171
  257.6 27.6 %reduce-scatter.8.cloned.1.call-done = f32[224,128]{1,0:T(8,128)} async-done(((f32[448,128]{1,0:T(8,128)}), f32[224,128]{1,0:T(8,128)}) %reduce-scatter.8.cloned.1.call-update) | async-done | bytes 114704 | tf_op jit(solution)/shard_map/reduce_scatter | solution.py:171
  285.2 12.2 %all_gather.12 = f32[448,128]{1,0:T(8,128)S(1)} all-gather(f32[224,128]{1,0:T(8,128)} %reduce-scatter.8.cloned.1.call-done), channel_id=1, replica_groups=mesh['dp_x'=4,'dp_z'=2,'dp_y'=4,'owner'=8] {'dp_z'}, dimensions={0}, use_global_device_ids=true | all-gather | bytes 344064 | tf_op jit(solution)/shard_map/all_gather | solution.py:174
  297.4 14.3 %all_gather.13 = f32[1792,128]{1,0:T(8,128)} all-gather(f32[448,128]{1,0:T(8,128)S(1)} %all_gather.12), channel_id=1, replica_groups=mesh['dp_x'=4,'dp_z'=2,'dp_y'=4,'owner'=8] {'dp_x'}, dimensions={0}, use_global_device_ids=true | all-gather | bytes 1146880 | tf_op jit(solution)/shard_map/all_gather | solution.py:174
  311.8 43.0 %all-gather.4.cloned.1.call-done = f32[7168,128]{1,0:T(8,128)} async-done(((f32[1792,128]{1,0:T(8,128)}), f32[7168,128]{1,0:T(8,128)}) %all-gather.4.cloned.1.call-update) | async-done | bytes 3670032 | tf_op jit(solution)/shard_map/all_gather | solution.py:174
  354.8 5.5 gather_fusion.2
  360.3 6.3 broadcast_multiply_fusion
  366.6 9.8 %copy.38 = f32[10,128,9,128]{1,0,3,2:T(8,128)} copy(f32[10,128,9,128]{3,1,2,0:T(8,128)} %bitcast.171) | data formatting | bytes 11796480 | tf_op jit(solution)/shard_map/mul | solution.py:107
  376.5 9.2 %copy.61 = f32[144,8,10,128]{3,1,2,0:T(8,128)} copy(f32[144,8,10,128]{3,2,1,0:T(8,128)} %bitcast.168) | data formatting | bytes 11796480
  385.6 7.7 copy.39
  394.2 11.7 %cholesky.165 = f32[128,128]{1,0:T(8,128)S(1)} custom-call(f32[128,128]{1,0:T(8,128)S(1)} %select_add_fusion.9), custom_call_target="Cholesky" | custom-call | tf_op jit(solution)/shard_map/jit(cholesky)/cholesky | solution.py:92
  407.9 9.8 %custom-call.16 = f32[1,128,128]{1,2,0:T(8,128)S(1)} custom-call(f32[1,128,128]{2,1,0:T(8,128)S(1)} %get-tuple-element.334), custom_call_target="InvertDiagBlocksLowerTriangular" | custom-call | tf_op jit(solution)/shard_map/triangular_solve/custom-call.0 | solution.py:94
  418.0 3.0 constant_dynamic-update-slice_fusion.46
  421.0 7.7 %constant_dynamic-update-slice_fusion.45 = (f32[1280,1152]{1,0:T(8,128)}, f32[1152,1024]{1,0:T(8,128)S(1)}) fusion(f32[1280,1152]{1,0:T(8,128)} %get-tuple-element.335, f32[1152,128]{1,0:T(8,128)S(1)} %get-tuple-element.336), kind=kOutput, calls=%fused_computation.236 | convolution fusion | flops 1814298624 | bytes 15269888 | tf_op jit(solution)/shard_map/dot_general | solution.py:86
  428.7 2.2 copy-done
  430.9 11.7 %cholesky.176 = f32[128,128]{1,0:T(8,128)S(1)} custom-call(f32[128,128]{1,0:T(8,128)S(1)} %select_add_fusion.8), custom_call_target="Cholesky" | custom-call | tf_op jit(solution)/shard_map/jit(cholesky)/cholesky | solution.py:92
  444.7 9.8 %custom-call.17 = f32[1,128,128]{1,2,0:T(8,128)S(1)} custom-call(f32[1,128,128]{2,1,0:T(8,128)S(1)} %get-tuple-element.332), custom_call_target="InvertDiagBlocksLowerTriangular" | custom-call | tf_op jit(solution)/shard_map/triangular_solve/custom-call.0 | solution.py:94
  454.8 2.5 constant_dynamic-update-slice_fusion.44
  457.3 6.2 constant_dynamic-update-slice_fusion.43
  463.6 1.8 copy-done.1
  465.4 11.7 %cholesky.187 = f32[128,128]{1,0:T(8,128)S(1)} custom-call(f32[128,128]{1,0:T(8,128)S(1)} %select_add_fusion.7), custom_call_target="Cholesky" | custom-call | tf_op jit(solution)/shard_map/jit(cholesky)/cholesky | solution.py:92
  479.2 9.8 %custom-call.18 = f32[1,128,128]{1,2,0:T(8,128)S(1)} custom-call(f32[1,128,128]{2,1,0:T(8,128)S(1)} %get-tuple-element.330), custom_call_target="InvertDiagBlocksLowerTriangular" | custom-call | tf_op jit(solution)/shard_map/triangular_solve/custom-call.0 | solution.py:94
  489.3 2.4 constant_dynamic-update-slice_fusion.42
  491.7 5.7 constant_dynamic-update-slice_fusion.41
  497.5 11.9 %cholesky.198 = f32[128,128]{1,0:T(8,128)S(1)} custom-call(f32[128,128]{1,0:T(8,128)S(1)} %select_add_fusion.6), custom_call_target="Cholesky" | custom-call | tf_op jit(solution)/shard_map/jit(cholesky)/cholesky | solution.py:92
  511.3 9.8 %custom-call.19 = f32[1,128,128]{1,2,0:T(8,128)S(1)} custom-call(f32[1,128,128]{2,1,0:T(8,128)S(1)} %get-tuple-element.328), custom_call_target="InvertDiagBlocksLowerTriangular" | custom-call | tf_op jit(solution)/shard_map/triangular_solve/custom-call.0 | solution.py:94
  522.7 4.6 constant_dynamic-update-slice_fusion.39
  527.4 11.7 %cholesky.209 = f32[128,128]{1,0:T(8,128)S(1)} custom-call(f32[128,128]{1,0:T(8,128)S(1)} %select_add_fusion.5), custom_call_target="Cholesky" | custom-call | tf_op jit(solution)/shard_map/jit(cholesky)/cholesky | solution.py:92
  541.1 9.8 %custom-call.20 = f32[1,128,128]{1,2,0:T(8,128)S(1)} custom-call(f32[1,128,128]{2,1,0:T(8,128)S(1)} %get-tuple-element.326), custom_call_target="InvertDiagBlocksLowerTriangular" | custom-call | tf_op jit(solution)/shard_map/triangular_solve/custom-call.0 | solution.py:94
  551.2 1.6 constant_dynamic-update-slice_fusion.38
  552.8 2.5 fusion.1
  556.6 11.7 %cholesky.220 = f32[128,128]{1,0:T(8,128)S(1)} custom-call(f32[128,128]{1,0:T(8,128)S(1)} %select_add_fusion.4), custom_call_target="Cholesky" | custom-call | tf_op jit(solution)/shard_map/jit(cholesky)/cholesky | solution.py:92
  570.2 9.8 %custom-call.21 = f32[1,128,128]{1,2,0:T(8,128)S(1)} custom-call(f32[1,128,128]{2,1,0:T(8,128)S(1)} %get-tuple-element.323), custom_call_target="InvertDiagBlocksLowerTriangular" | custom-call | tf_op jit(solution)/shard_map/triangular_solve/custom-call.0 | solution.py:94
  581.4 1.9 fusion.2
  585.3 11.9 %cholesky.264 = f32[128,128]{1,0:T(8,128)S(1)} custom-call(f32[128,128]{1,0:T(8,128)S(1)} %select_add_fusion), custom_call_target="Cholesky" | custom-call | tf_op jit(solution)/shard_map/jit(cholesky)/cholesky | solution.py:92
  598.5 9.8 %custom-call.25 = f32[1,128,128]{1,2,0:T(8,128)S(1)} custom-call(f32[1,128,128]{2,1,0:T(8,128)S(1)} %fusion.72), custom_call_target="InvertDiagBlocksLowerTriangular" | custom-call | tf_op jit(solution)/shard_map/triangular_solve/custom-call.0 | solution.py:94
  608.6 11.7 %cholesky.231 = f32[128,128]{1,0:T(8,128)S(1)} custom-call(f32[128,128]{1,0:T(8,128)S(1)} %select_add_fusion.3), custom_call_target="Cholesky" | custom-call | tf_op jit(solution)/shard_map/jit(cholesky)/cholesky | solution.py:92
  622.3 9.8 %custom-call.22 = f32[1,128,128]{1,2,0:T(8,128)S(1)} custom-call(f32[1,128,128]{2,1,0:T(8,128)S(1)} %get-tuple-element.321), custom_call_target="InvertDiagBlocksLowerTriangular" | custom-call | tf_op jit(solution)/shard_map/triangular_solve/custom-call.0 | solution.py:94
  633.4 1.5 fusion.3
  634.9 11.9 %cholesky.242 = f32[128,128]{1,0:T(8,128)S(1)} custom-call(f32[128,128]{1,0:T(8,128)S(1)} %select_add_fusion.2), custom_call_target="Cholesky" | custom-call | tf_op jit(solution)/shard_map/jit(cholesky)/cholesky | solution.py:92
  648.2 9.8 %custom-call.23 = f32[1,128,128]{1,2,0:T(8,128)S(1)} custom-call(f32[1,128,128]{2,1,0:T(8,128)S(1)} %fusion.70), custom_call_target="InvertDiagBlocksLowerTriangular" | custom-call | tf_op jit(solution)/shard_map/triangular_solve/custom-call.0 | solution.py:94
  658.9 11.7 %cholesky.253 = f32[128,128]{1,0:T(8,128)S(1)} custom-call(f32[128,128]{1,0:T(8,128)S(1)} %select_add_fusion.1), custom_call_target="Cholesky" | custom-call | tf_op jit(solution)/shard_map/jit(cholesky)/cholesky | solution.py:92
  671.9 9.8 %custom-call.24 = f32[1,128,128]{1,2,0:T(8,128)S(1)} custom-call(f32[1,128,128]{2,1,0:T(8,128)S(1)} %fusion.71), custom_call_target="InvertDiagBlocksLowerTriangular" | custom-call | tf_op jit(solution)/shard_map/triangular_solve/custom-call.0 | solution.py:94
  685.9 1.6 convolution_subtract_fusion.6
  687.8 1.7 convolution_subtract_fusion.3
  689.8 1.8 convolution_subtract_fusion.2
  692.0 1.9 convolution_subtract_fusion.1
  694.3 2.1 convolution_subtract_fusion
  698.9 60.0 %all-gather.6.cloned.1.call-done = f32[9216,128]{1,0:T(8,128)} async-done(((f32[1152,128]{1,0:T(8,128)}), f32[9216,128]{1,0:T(8,128)}) %all-gather.6.cloned.1.call-update) | async-done | bytes 4718608 | tf_op jit(solution)/shard_map/all_gather | solution.py:177
  758.9 4.9 copy.113
  (134 shorter events, 41.0 us)
Async XLA Ops:
  7.8 16.9 %all-to-all-start = ((s32[8,1,4]{2,1,0:T(1,128)}), s32[8,1,4]{2,1,0:T(1,128)S(1)}, u32[]{:S(2)}, u32[]{:S(2)}) async-start(s32[8,1,4]{2,1,0:T(1,128)} %broadcast_in_dim.67), calls=%async_computation | async-start | bytes 8192 | tf_op jit(solution)/shard_map/all_to_all | solution.py:153
  24.7 99.2 %all-to-all-start.1 = ((bf16[8,512,512]{2,1,0:T(8,128)(2,1)}), bf16[8,512,512]{2,1,0:T(8,128)(2,1)}, u32[]{:S(2)}, u32[]{:S(2)}) async-start(bf16[8,512,512]{2,1,0:T(8,128)(2,1)} %broadcast_select_fusion), calls=%async_computation.1 | async-start | bytes 8388608 | tf_op jit(solution)/shard_map/all_to_all | solution.py:152
  29.8 202.2 %reduce-scatter.4.cloned.1.call-start = ((), (), s32[]{:S(2)}) async-start(), calls=%async_computation.5 | async-start | bytes 4587520 | tf_op jit(solution)/shard_map/reduce_scatter | solution.py:171
  153.9 22.7 %copy-start.2 = (s32[55]{0:T(128)S(1)}, s32[55]{0:T(128)}, u32[]{:S(2)}) copy-start(s32[55]{0:T(128)} %constant.760) | copy-start | bytes 664
  182.0 129.7 %copy-start.3 = (s32[90]{0:T(128)S(1)}, s32[90]{0:T(128)}, u32[]{:S(2)}) copy-start(s32[90]{0:T(128)} %constant.761) | copy-start | bytes 1084
  186.4 71.1 %reduce-scatter.6.cloned.1.call-start = ((), (), s32[]{:S(2)}) async-start(), calls=%async_computation.6 | async-start | bytes 1146880 | tf_op jit(solution)/shard_map/reduce_scatter | solution.py:171
  232.0 53.2 %reduce-scatter.8.cloned.1.call-start = ((), (), s32[]{:S(2)}) async-start(), calls=%async_computation.7 | async-start | bytes 344064 | tf_op jit(solution)/shard_map/reduce_scatter | solution.py:171
  257.5 97.3 %all-gather.4.cloned.1.call-start = ((), (), s32[]{:S(2)}) async-start(), calls=%async_computation.8 | async-start | bytes 4587520 | tf_op jit(solution)/shard_map/all_gather | solution.py:174
  311.7 447.2 %all-gather.6.cloned.1.call-start = ((), (), s32[]{:S(2)}) async-start(), calls=%async_computation.9 | async-start | bytes 5308416 | tf_op jit(solution)/shard_map/all_gather | solution.py:177
  428.7 2.2 copy-start
  463.5 1.8 copy-start.1
Sparse Core Ops, SparseCore 0:
  186.5 45.4 reduce-scatter.3
  234.6 22.9 reduce-scatter.5
  260.0 25.1 reduce-scatter.7
  311.8 42.9 all-gather.3
  699.0 59.8 all-gather.5
where the time goes:
time: 780 us; the launch traced here: 771 us
  waiting for transfers between devices  295 us (38%)
  other arithmetic  256 us (33%)
  matrix products  85.5 us (11%)
  local copies, waits for them, and re-layouts  81.5 us (10%)
  blocking collectives  26.5 us (3%)
  between operations  14.3 us (2%)
  starting transfers between devices  11.2 us (1%)
    another operation x30, other arithmetic, _chol_inv(): lower = jnp.linalg.cholesky(block, symmetrize_input=False)  125 us
    another operation x15, other arithmetic, _chol_inv(): lax.linalg.triangular_solve(lower, eye, left_side=True, lower=True)  103 us
    reduce_scatter x3, waiting for transfers between devices, body(): mine = lax.psum_scatter(mine, axis, scatter_dimension=0, tiled=True)  98.6 us
    all_to_all x1, waiting for transfers between devices, body(): lax.all_to_all(ordered, 'owner', split_axis=0, concat_axis=1, tiled=True)  93.7 us
    all_gather x1, waiting for transfers between devices, body(): return lax.all_gather(results, 'owner', axis=0, tiled=True)  60 us
    dot_general x18, matrix products, _mm_nt(): lax.dot_general(a, b, (((1,), (1,)), ((), ())), precision=HIGH, preferred...  44.6 us
    all_gather x1, waiting for transfers between devices, body(): gathered = lax.all_gather(gathered, axis, axis=0, tiled=True)  43 us
    all_gather x2, blocking collectives, body(): gathered = lax.all_gather(gathered, axis, axis=0, tiled=True)  26.5 us
  transfers between devices with their start and end apart: 7, of which 6 were waited for; matrix products, arithmetic and copies ran while one was open for 1% of the time, Pallas kernels for 0%

commit v1 on v0

--- a/solution.py
+++ b/solution.py
@@ -174,7 +174,14 @@
         gathered = lax.all_gather(gathered, axis, axis=0, tiled=True)
     gathered = gathered.reshape(padded, block, block)
     results = precondition_blocks(gathered, nb, total_rows)[None]
-    return lax.all_gather(results, "owner", axis=0, tiled=True)
+
+    def shape_shelves_for(mesh_ax, local):
+        state_now = jax.lax.axis_size(mesh_ax)
+        outcome_arr = jnp.stack([local] * state_now, axis=0)
+        y = jax.lax.all_to_all(outcome_arr, axis_name=mesh_ax, split_axis=0, concat_axis=0)
+        return jnp.concatenate(y, axis=0)
+
+    return shape_shelves_for("owner", results)
 
 
 DP_AXES = ("dp_x", "dp_z", "dp_y")

time: 780 us -> 827 us (1.060)
  blocking collectives: 26.5 us -> 136 us
  waiting for transfers between devices: 295 us -> 235 us
    all_to_all x0 -> x1, blocking collectives: none -> 110 us  [shape_shelves_for(): jax.lax.all_to_all(outcome_arr, axis_name=mesh_ax, split_axis=0, concat_a...]
    all_gather x1 -> x0, waiting for transfers between devices: 60 us -> none  [body(): return lax.all_gather(results, 'owner', axis=0, tiled=True)]
  transfers between devices with their start and end apart: 7 -> 6, of which waited for: 6 -> 5; matrix products, arithmetic and copies ran while one was open for 1% -> 1% of each run, Pallas kernels for 0% -> 0%
where the time goes in v1:
time: 827 us; the launch traced here: 817 us
  other arithmetic  256 us (31%)
  waiting for transfers between devices  235 us (28%)
  blocking collectives  136 us (16%)
  matrix products  84.7 us (10%)
  local copies, waits for them, and re-layouts  79.2 us (10%)
  between operations  14.3 us (2%)
  starting transfers between devices  11.2 us (1%)
    another operation x30, other arithmetic, _chol_inv(): lower = jnp.linalg.cholesky(block, symmetrize_input=False)  125 us
    all_to_all x1, blocking collectives, shape_shelves_for(): jax.lax.all_to_all(outcome_arr, axis_name=mesh_ax, split_axis=0, concat_a...  110 us
    another operation x15, other arithmetic, _chol_inv(): lax.linalg.triangular_solve(lower, eye, left_side=True, lower=True)  103 us
    reduce_scatter x3, waiting for transfers between devices, body(): mine = lax.psum_scatter(mine, axis, scatter_dimension=0, tiled=True)  98.6 us
    all_to_all x1, waiting for transfers between devices, body(): lax.all_to_all(ordered, 'owner', split_axis=0, concat_axis=1, tiled=True)  93.7 us
    dot_general x18, matrix products, _mm_nt(): lax.dot_general(a, b, (((1,), (1,)), ((), ())), precision=HIGH, preferred...  44.6 us
    all_gather x1, waiting for transfers between devices, body(): gathered = lax.all_gather(gathered, axis, axis=0, tiled=True)  43.1 us
    all_gather x2, blocking collectives, body(): gathered = lax.all_gather(gathered, axis, axis=0, tiled=True)  26.5 us
  transfers between devices with their start and end apart: 6, of which 5 were waited for; matrix products, arithmetic and copies ran while one was open for 1% of the time, Pallas kernels for 0%

profile of v1, /device:TPU:2, one launch (start us, length us, event | category | flops | bytes accessed | tf_op | source)
XLA Modules:
  0.0 817.5 jit_solution(11178087590433460996)
XLA Ops:
  7.8 5.9 all-to-all-start
  15.0 5.0 gather_fusion
  20.0 4.7 broadcast_select_fusion
  24.7 5.1 all-to-all-start.1
  30.2 93.7 %all-to-all-done.1 = bf16[8,512,512]{2,1,0:T(8,128)(2,1)} async-done(((bf16[8,512,512]{2,1,0:T(8,128)(2,1)}), bf16[8,512,512]{2,1,0:T(8,128)(2,1)}, u32[]{:S(2)}, u32[]{:S(2)}) %all-to-all-start.1) | async-done | bytes 4194336 | tf_op jit(solution)/shard_map/all_to_all | solution.py:152
  125.2 2.3 slice.830
  127.5 3.9 fusion.101
  131.3 2.2 pad_select_fusion
  133.6 6.0 fusion
  139.5 14.3 %copy.37 = bf16[1280,4096]{1,0:T(8,128)(2,1)} copy(bf16[1280,4096]{0,1:T(8,128)(2,1)} %fusion) | data formatting | bytes 20971520 | tf_op jit(solution)/shard_map/dot_general | solution.py:158
  153.9 22.7 %convolution_bitcast_fusion = f32[10,10,128,128]{3,2,1,0:T(8,128)} fusion(bf16[10,128,4096,1]{2,1,3,0:T(8,128)(2,1)} %bitcast.177, bf16[10,128,4096,1]{2,1,0,3:T(8,128)(2,1)} %bitcast.178), kind=kOutput, calls=%fused_computation.13 | convolution fusion | flops 13421772800 | bytes 27525120 | tf_op jit(solution)/shard_map/dot_general | solution.py:158
  176.6 5.5 gather_fusion.1
  182.0 4.3 concatenate.110
  186.4 45.5 %reduce-scatter.4.cloned.1.call-done = f32[1792,128]{1,0:T(8,128)} async-done(((f32[7168,128]{1,0:T(8,128)}), f32[1792,128]{1,0:T(8,128)}) %reduce-scatter.4.cloned.1.call-update) | async-done | bytes 917520 | tf_op jit(solution)/shard_map/reduce_scatter | solution.py:171
  232.1 25.5 %reduce-scatter.6.cloned.1.call-done = f32[448,128]{1,0:T(8,128)} async-done(((f32[1792,128]{1,0:T(8,128)}), f32[448,128]{1,0:T(8,128)}) %reduce-scatter.6.cloned.1.call-update) | async-done | bytes 229392 | tf_op jit(solution)/shard_map/reduce_scatter | solution.py:171
  257.6 27.6 %reduce-scatter.8.cloned.1.call-done = f32[224,128]{1,0:T(8,128)} async-done(((f32[448,128]{1,0:T(8,128)}), f32[224,128]{1,0:T(8,128)}) %reduce-scatter.8.cloned.1.call-update) | async-done | bytes 114704 | tf_op jit(solution)/shard_map/reduce_scatter | solution.py:171
  285.2 12.2 %all_gather.9 = f32[448,128]{1,0:T(8,128)S(1)} all-gather(f32[224,128]{1,0:T(8,128)} %reduce-scatter.8.cloned.1.call-done), channel_id=1, replica_groups=mesh['dp_x'=4,'dp_z'=2,'dp_y'=4,'owner'=8] {'dp_z'}, dimensions={0}, use_global_device_ids=true | all-gather | bytes 344064 | tf_op jit(solution)/shard_map/all_gather | solution.py:174
  297.4 14.3 %all_gather.10 = f32[1792,128]{1,0:T(8,128)} all-gather(f32[448,128]{1,0:T(8,128)S(1)} %all_gather.9), channel_id=1, replica_groups=mesh['dp_x'=4,'dp_z'=2,'dp_y'=4,'owner'=8] {'dp_x'}, dimensions={0}, use_global_device_ids=true | all-gather | bytes 1146880 | tf_op jit(solution)/shard_map/all_gather | solution.py:174
  311.7 43.1 %all-gather.2.cloned.1.call-done = f32[7168,128]{1,0:T(8,128)} async-done(((f32[1792,128]{1,0:T(8,128)}), f32[7168,128]{1,0:T(8,128)}) %all-gather.2.cloned.1.call-update) | async-done | bytes 3670032 | tf_op jit(solution)/shard_map/all_gather | solution.py:174
  354.8 5.5 gather_fusion.2
  360.3 6.3 broadcast_multiply_fusion
  366.6 9.8 %copy.38 = f32[10,128,9,128]{1,0,3,2:T(8,128)} copy(f32[10,128,9,128]{3,1,2,0:T(8,128)} %bitcast.171) | data formatting | bytes 11796480 | tf_op jit(solution)/shard_map/mul | solution.py:107
  376.5 9.2 %copy.61 = f32[144,8,10,128]{3,1,2,0:T(8,128)} copy(f32[144,8,10,128]{3,2,1,0:T(8,128)} %bitcast.168) | data formatting | bytes 11796480
  385.6 7.7 copy.39
  394.2 11.7 %cholesky.165 = f32[128,128]{1,0:T(8,128)S(1)} custom-call(f32[128,128]{1,0:T(8,128)S(1)} %select_add_fusion.9), custom_call_target="Cholesky" | custom-call | tf_op jit(solution)/shard_map/jit(cholesky)/cholesky | solution.py:92
  407.9 9.8 %custom-call.16 = f32[1,128,128]{1,2,0:T(8,128)S(1)} custom-call(f32[1,128,128]{2,1,0:T(8,128)S(1)} %get-tuple-element.334), custom_call_target="InvertDiagBlocksLowerTriangular" | custom-call | tf_op jit(solution)/shard_map/triangular_solve/custom-call.0 | solution.py:94
  418.0 3.0 constant_dynamic-update-slice_fusion.46
  421.0 7.7 constant_dynamic-update-slice_fusion.45
  428.7 2.2 copy-done
  430.9 11.7 %cholesky.176 = f32[128,128]{1,0:T(8,128)S(1)} custom-call(f32[128,128]{1,0:T(8,128)S(1)} %select_add_fusion.8), custom_call_target="Cholesky" | custom-call | tf_op jit(solution)/shard_map/jit(cholesky)/cholesky | solution.py:92
  444.7 9.8 %custom-call.17 = f32[1,128,128]{1,2,0:T(8,128)S(1)} custom-call(f32[1,128,128]{2,1,0:T(8,128)S(1)} %get-tuple-element.332), custom_call_target="InvertDiagBlocksLowerTriangular" | custom-call | tf_op jit(solution)/shard_map/triangular_solve/custom-call.0 | solution.py:94
  454.8 2.5 constant_dynamic-update-slice_fusion.44
  457.3 6.2 constant_dynamic-update-slice_fusion.43
  463.6 1.8 copy-done.1
  465.4 11.7 %cholesky.187 = f32[128,128]{1,0:T(8,128)S(1)} custom-call(f32[128,128]{1,0:T(8,128)S(1)} %select_add_fusion.7), custom_call_target="Cholesky" | custom-call | tf_op jit(solution)/shard_map/jit(cholesky)/cholesky | solution.py:92
  479.2 9.8 %custom-call.18 = f32[1,128,128]{1,2,0:T(8,128)S(1)} custom-call(f32[1,128,128]{2,1,0:T(8,128)S(1)} %get-tuple-element.330), custom_call_target="InvertDiagBlocksLowerTriangular" | custom-call | tf_op jit(solution)/shard_map/triangular_solve/custom-call.0 | solution.py:94
  489.3 2.4 constant_dynamic-update-slice_fusion.42
  491.7 5.7 constant_dynamic-update-slice_fusion.41
  497.5 11.9 %cholesky.198 = f32[128,128]{1,0:T(8,128)S(1)} custom-call(f32[128,128]{1,0:T(8,128)S(1)} %select_add_fusion.6), custom_call_target="Cholesky" | custom-call | tf_op jit(solution)/shard_map/jit(cholesky)/cholesky | solution.py:92
  511.3 9.8 %custom-call.19 = f32[1,128,128]{1,2,0:T(8,128)S(1)} custom-call(f32[1,128,128]{2,1,0:T(8,128)S(1)} %get-tuple-element.328), custom_call_target="InvertDiagBlocksLowerTriangular" | custom-call | tf_op jit(solution)/shard_map/triangular_solve/custom-call.0 | solution.py:94
  522.7 4.6 constant_dynamic-update-slice_fusion.39
  527.4 11.7 %cholesky.209 = f32[128,128]{1,0:T(8,128)S(1)} custom-call(f32[128,128]{1,0:T(8,128)S(1)} %select_add_fusion.5), custom_call_target="Cholesky" | custom-call | tf_op jit(solution)/shard_map/jit(cholesky)/cholesky | solution.py:92
  541.1 9.8 %custom-call.20 = f32[1,128,128]{1,2,0:T(8,128)S(1)} custom-call(f32[1,128,128]{2,1,0:T(8,128)S(1)} %get-tuple-element.326), custom_call_target="InvertDiagBlocksLowerTriangular" | custom-call | tf_op jit(solution)/shard_map/triangular_solve/custom-call.0 | solution.py:94
  551.2 1.6 constant_dynamic-update-slice_fusion.38
  552.8 2.5 fusion.1
  556.6 11.7 %cholesky.220 = f32[128,128]{1,0:T(8,128)S(1)} custom-call(f32[128,128]{1,0:T(8,128)S(1)} %select_add_fusion.4), custom_call_target="Cholesky" | custom-call | tf_op jit(solution)/shard_map/jit(cholesky)/cholesky | solution.py:92
  570.2 9.8 %custom-call.21 = f32[1,128,128]{1,2,0:T(8,128)S(1)} custom-call(f32[1,128,128]{2,1,0:T(8,128)S(1)} %get-tuple-element.323), custom_call_target="InvertDiagBlocksLowerTriangular" | custom-call | tf_op jit(solution)/shard_map/triangular_solve/custom-call.0 | solution.py:94
  581.4 1.9 fusion.2
  585.3 11.9 %cholesky.264 = f32[128,128]{1,0:T(8,128)S(1)} custom-call(f32[128,128]{1,0:T(8,128)S(1)} %select_add_fusion), custom_call_target="Cholesky" | custom-call | tf_op jit(solution)/shard_map/jit(cholesky)/cholesky | solution.py:92
  598.5 9.8 %custom-call.25 = f32[1,128,128]{1,2,0:T(8,128)S(1)} custom-call(f32[1,128,128]{2,1,0:T(8,128)S(1)} %fusion.72), custom_call_target="InvertDiagBlocksLowerTriangular" | custom-call | tf_op jit(solution)/shard_map/triangular_solve/custom-call.0 | solution.py:94
  608.6 11.7 %cholesky.231 = f32[128,128]{1,0:T(8,128)S(1)} custom-call(f32[128,128]{1,0:T(8,128)S(1)} %select_add_fusion.3), custom_call_target="Cholesky" | custom-call | tf_op jit(solution)/shard_map/jit(cholesky)/cholesky | solution.py:92
  622.3 9.8 %custom-call.22 = f32[1,128,128]{1,2,0:T(8,128)S(1)} custom-call(f32[1,128,128]{2,1,0:T(8,128)S(1)} %get-tuple-element.321), custom_call_target="InvertDiagBlocksLowerTriangular" | custom-call | tf_op jit(solution)/shard_map/triangular_solve/custom-call.0 | solution.py:94
  633.4 1.5 fusion.3
  634.9 11.9 %cholesky.242 = f32[128,128]{1,0:T(8,128)S(1)} custom-call(f32[128,128]{1,0:T(8,128)S(1)} %select_add_fusion.2), custom_call_target="Cholesky" | custom-call | tf_op jit(solution)/shard_map/jit(cholesky)/cholesky | solution.py:92
  648.2 9.8 %custom-call.23 = f32[1,128,128]{1,2,0:T(8,128)S(1)} custom-call(f32[1,128,128]{2,1,0:T(8,128)S(1)} %fusion.70), custom_call_target="InvertDiagBlocksLowerTriangular" | custom-call | tf_op jit(solution)/shard_map/triangular_solve/custom-call.0 | solution.py:94
  658.9 11.7 %cholesky.253 = f32[128,128]{1,0:T(8,128)S(1)} custom-call(f32[128,128]{1,0:T(8,128)S(1)} %select_add_fusion.1), custom_call_target="Cholesky" | custom-call | tf_op jit(solution)/shard_map/jit(cholesky)/cholesky | solution.py:92
  671.9 9.8 %custom-call.24 = f32[1,128,128]{1,2,0:T(8,128)S(1)} custom-call(f32[1,128,128]{2,1,0:T(8,128)S(1)} %fusion.71), custom_call_target="InvertDiagBlocksLowerTriangular" | custom-call | tf_op jit(solution)/shard_map/triangular_solve/custom-call.0 | solution.py:94
  685.9 1.6 convolution_subtract_fusion.6
  687.8 1.7 convolution_subtract_fusion.3
  689.8 1.8 convolution_subtract_fusion.2
  692.0 1.9 convolution_subtract_fusion.1
  694.3 2.1 convolution_subtract_fusion
  698.4 109.9 %all_to_all.23 = f32[8,1,1152,128]{3,2,1,0:T(8,128)S(1)} all-to-all(f32[8,1,1152,128]{3,2,1,0:T(8,128)S(1)} %stack.3), channel_id=1, replica_groups=mesh['dp_x'=4,'dp_z'=2,'dp_y'=4,'owner'=8] {'owner'}, dimensions={0} | all-to-all | bytes 9437184 | tf_op jit(solution)/shard_map/all_to_all | solution.py:181
  808.3 2.2 copy.113
  (133 shorter events, 40.4 us)
Async XLA Ops:
  7.8 16.9 %all-to-all-start = ((s32[8,1,4]{2,1,0:T(1,128)}), s32[8,1,4]{2,1,0:T(1,128)S(1)}, u32[]{:S(2)}, u32[]{:S(2)}) async-start(s32[8,1,4]{2,1,0:T(1,128)} %broadcast_in_dim.64), calls=%async_computation | async-start | bytes 8192 | tf_op jit(solution)/shard_map/all_to_all | solution.py:153
  24.7 99.2 %all-to-all-start.1 = ((bf16[8,512,512]{2,1,0:T(8,128)(2,1)}), bf16[8,512,512]{2,1,0:T(8,128)(2,1)}, u32[]{:S(2)}, u32[]{:S(2)}) async-start(bf16[8,512,512]{2,1,0:T(8,128)(2,1)} %broadcast_select_fusion), calls=%async_computation.1 | async-start | bytes 8388608 | tf_op jit(solution)/shard_map/all_to_all | solution.py:152
  29.8 202.2 %reduce-scatter.4.cloned.1.call-start = ((), (), s32[]{:S(2)}) async-start(), calls=%async_computation.6 | async-start | bytes 4587520 | tf_op jit(solution)/shard_map/reduce_scatter | solution.py:171
  153.9 22.7 %copy-start.2 = (s32[55]{0:T(128)S(1)}, s32[55]{0:T(128)}, u32[]{:S(2)}) copy-start(s32[55]{0:T(128)} %constant.760) | copy-start | bytes 664
  182.0 129.7 %copy-start.3 = (s32[90]{0:T(128)S(1)}, s32[90]{0:T(128)}, u32[]{:S(2)}) copy-start(s32[90]{0:T(128)} %constant.761) | copy-start | bytes 1084
  186.4 71.1 %reduce-scatter.6.cloned.1.call-start = ((), (), s32[]{:S(2)}) async-start(), calls=%async_computation.7 | async-start | bytes 1146880 | tf_op jit(solution)/shard_map/reduce_scatter | solution.py:171
  232.0 53.2 %reduce-scatter.8.cloned.1.call-start = ((), (), s32[]{:S(2)}) async-start(), calls=%async_computation.8 | async-start | bytes 344064 | tf_op jit(solution)/shard_map/reduce_scatter | solution.py:171
  257.5 97.3 %all-gather.2.cloned.1.call-start = ((), (), s32[]{:S(2)}) async-start(), calls=%async_computation.9 | async-start | bytes 4587520 | tf_op jit(solution)/shard_map/all_gather | solution.py:174
  428.7 2.2 copy-start
  463.5 1.8 copy-start.1
Sparse Core Ops, SparseCore 0:
  186.5 45.4 reduce-scatter.3
  234.6 22.9 reduce-scatter.5
  260.0 25.1 reduce-scatter.7
  311.8 42.9 all-gather.1
